TPU v7x, 32 devices: a whole 2x2x4 slice. The times are simulated.
32 devices in a mesh: lat: 8 (over y, x, core), lon: 4 (over z).
Axes of the slice: x: 2, y: 2, z: 4, core: 2. Of those that a mesh axis runs over, the one named last changes fastest.
Arguments:
- features: bfloat16 [192, 180, 256], P('lat', 'lon'), may hold values from -6 to 6
- obs_mask: int32 [192, 180, 8], P('lat', 'lon'), may hold values 0 or 1
- filter_taps: bfloat16 [192, 4, 3, 17], replicated, may hold values from 0.049804688 to 1
- band_width: int32 [192], replicated, may hold values from 1 to 8, as said below
- mixing: bfloat16 [8, 4, 32, 32], replicated, may hold values from -0.5 to 0.5
- cotangent: bfloat16 [192, 180, 256], P('lat', 'lon'), may hold values from -6 to 6
Outputs:
- infilled: bfloat16 [192, 180, 256], P('lat', 'lon')
- input_grad: bfloat16 [192, 180, 256], P('lat', 'lon')
- weight_grad: float32 [8, 4, 32, 32], replicated
Inputs may be any that keep to these rules, and one draw needn't show every extreme that they name: band_width is 8 at the first and last cycle and 1 at cycle 192 // 2.
All inputs are finite; a program needn't handle non-finite values. No bound on the sum of `obs_mask` on one device may be relied on, other than what follows from the above.
Results may differ from a plain program's by a relative error of at most 0.005.
Values may be sent and summed in bfloat16 or wider, within the bound.
No kernel may reach another device: no remote copies, remote signals or barrier semaphores. Data moves between devices by JAX's collectives and lax.ppermute only.
A program may use at most 128 MiB of HBM per device.

v0:
```python
import math
import jax
import jax.numpy as jnp
from jax import lax
from jax.sharding import PartitionSpec as P


def with_halo(block, sides, width, periodic):
    for axis, dim in sides:
        count = lax.axis_size(axis)
        forward = [(i, i + 1) for i in range(count - 1)]
        if periodic:
            forward.append((count - 1, 0))
        backward = [(target, source) for source, target in forward]
        low = lax.ppermute(
            lax.slice_in_dim(block, block.shape[dim] - width, None, axis=dim), axis, forward
        )
        high = lax.ppermute(lax.slice_in_dim(block, 0, width, axis=dim), axis, backward)
        block = jnp.concatenate([low, block, high], axis=dim)
    return block


def passed_along(block, axis, distance):
    devices = range(lax.axis_size(axis))
    route = [(i - distance, i) for i in devices if i - distance in devices]
    return lax.ppermute(block, axis, route)


def from_behind(x, axis, by):
    size = lax.axis_size(axis)
    return lax.ppermute(x, axis, [(i, (i + by) % size) for i in range(size)])


def local(features, obs_mask, filter_taps, band_width, mixing, cotangent):
    row_count, col_count, chan_count = features.shape
    group_count = obs_mask.shape[2]
    group_width = chan_count // group_count
    basis_count = mixing.shape[1]
    tap_count = filter_taps.shape[3]
    tap_reach = (tap_count - 1) // 2
    padded_cols = col_count + 2 * tap_reach
    mask_values = obs_mask.astype(jnp.bfloat16)
    masked = (
        features.reshape(row_count, col_count, group_count, group_width) * mask_values[..., None]
    ).reshape(row_count, col_count, chan_count)
    wide_input, wide_mask = (
        with_halo(masked, (("lon", 1),), tap_reach, True),
        with_halo(mask_values, (("lon", 1),), tap_reach, True),
    )
    full_input, full_mask = (
        with_halo(wide_input, (("lat", 0),), 1, False),
        with_halo(wide_mask, (("lat", 0),), 1, False),
    )
    offsets = jnp.arange(tap_count) - tap_reach
    allowed = jnp.abs(offsets)[None, :] <= band_width[:, None]
    global_taps = filter_taps * allowed[:, None, None, :].astype(jnp.bfloat16)
    first_row = lax.axis_index("lat") * row_count
    local_taps = lax.dynamic_slice_in_dim(global_taps, first_row, row_count, 0)
    padded_index = jnp.arange(padded_cols)
    output_index = jnp.arange(col_count)
    tap_index = jnp.arange(tap_count)
    forward_table = (
        padded_index[None, :, None] - output_index[None, None, :] == tap_index[:, None, None]
    ).astype(jnp.bfloat16)
    band_blocks = jnp.einsum(
        "ibed,dpj->ibepj", local_taps, forward_table, preferred_element_type=jnp.float32
    ).astype(jnp.bfloat16)
    numerator = jnp.zeros((row_count, basis_count, col_count, chan_count), jnp.float32)
    denominator = jnp.zeros((row_count, basis_count, col_count, group_count), jnp.float32)
    for lat_step in range(3):
        band_block = band_blocks[:, :, lat_step]
        numerator = numerator + jnp.einsum(
            "ibpj,ipc->ibjc",
            band_block,
            full_input[lat_step : lat_step + row_count],
            preferred_element_type=jnp.float32,
        )
        denominator = denominator + jnp.einsum(
            "ibpj,ipg->ibjg",
            band_block,
            full_mask[lat_step : lat_step + row_count],
            preferred_element_type=jnp.float32,
        )
    safe_denom = jnp.maximum(denominator, 1.0)
    scaled = (
        numerator.reshape(row_count, basis_count, col_count, group_count, group_width)
        / safe_denom[..., None]
    ).astype(jnp.bfloat16)
    infilled = (
        jnp.einsum("ibjgc,gbco->ijgo", scaled, mixing, preferred_element_type=jnp.float32)
        .reshape(row_count, col_count, chan_count)
        .astype(jnp.bfloat16)
    )
    upstream = cotangent.reshape(row_count, col_count, group_count, group_width)
    local_grad = jnp.einsum(
        "ibjgc,ijgo->gbco", scaled, upstream, preferred_element_type=jnp.float32
    )
    cell_count = row_count * lax.axis_size("lat") * col_count * lax.axis_size("lon")
    weight_grad = lax.psum(local_grad, ("lat", "lon")) * (1.0 / math.sqrt(cell_count))
    back_prop = jnp.einsum("ijgo,gbco->ibjgc", upstream, mixing, preferred_element_type=jnp.float32)
    pulled = (
        (back_prop / safe_denom[..., None])
        .astype(jnp.bfloat16)
        .reshape(row_count, basis_count, col_count, chan_count)
    )
    collected = jnp.zeros((row_count + 2, padded_cols, chan_count), jnp.float32)
    for lat_step in range(3):
        term_rows = jnp.einsum(
            "ibpj,ibjc->ipc",
            band_blocks[:, :, lat_step],
            pulled,
            preferred_element_type=jnp.float32,
        )
        collected = collected.at[lat_step : lat_step + row_count].add(term_rows)
    from_below = passed_along(collected[0:1], "lat", -1)
    from_above = passed_along(collected[row_count + 1 : row_count + 2], "lat", 1)
    inner_rows = collected[1 : row_count + 1]
    inner_rows = inner_rows.at[row_count - 1 : row_count].add(from_below)
    inner_rows = inner_rows.at[0:1].add(from_above)
    left_rim = inner_rows[:, :tap_reach]
    right_rim = inner_rows[:, col_count + tap_reach :]
    from_right = from_behind(left_rim.astype(jnp.bfloat16), "lon", -1).astype(left_rim.dtype)
    from_left = from_behind(right_rim, "lon", 1)
    gathered = inner_rows[:, tap_reach : tap_reach + col_count]
    gathered = gathered.at[:, col_count - tap_reach :].add(from_right)
    gathered = gathered.at[:, :tap_reach].add(from_left)
    input_grad = (
        (gathered.reshape(row_count, col_count, group_count, group_width) * mask_values[..., None])
        .reshape(row_count, col_count, chan_count)
        .astype(jnp.bfloat16)
    )
    return (infilled, input_grad, weight_grad)


def solution(mesh):
    placed = (P("lat", "lon", None), P("lat", "lon", None), P(), P(), P(), P("lat", "lon", None))
    return jax.shard_map(
        local,
        mesh=mesh,
        in_specs=placed,
        out_specs=(P("lat", "lon", None), P("lat", "lon", None), P()),
        check_vma=False,
    )
```

profile of v0, /device:TPU:0, one launch (start us, length us, event | category | flops | bytes accessed | tf_op | source)
XLA Modules:
  0.0 297.3 jit_solution(17708958694991090387)
XLA Ops:
  7.2 0.9 convert_element_type.43
  8.2 3.1 %collective-permute-start.4 = (bf16[24,8,8]{1,2,0:T(8,128)(2,1)S(1)}, bf16[24,8,8]{1,2,0:T(8,128)(2,1)S(1)}, u32[]{:S(2)}, u32[]{:S(2)}) collective-permute-start(bf16[24,8,8]{1,2,0:T(8,128)(2,1)S(1)} %get-tuple-element.109), channel_id=1, source_target_pairs={{0,1},{1,2},{2,3},{3,0},{4,5},{5,6},{6,7},{7,4},{8,9},{9,10},{10,1... | collective-permute-start | bytes 9224 | tf_op jit(solution)/shard_map/ppermute | solution.py:15
  11.3 2.1 collective-permute-start.5
  13.7 0.8 compare_convert_fusion
  14.6 1.0 constant_dynamic-slice_fusion
  15.8 1.4 mul.42
  17.2 2.3 mul.43
  19.5 1.0 convolution_convert_fusion
  20.5 1.6 slice_bitcast_fusion
  22.3 3.9 %reshape.274 = bf16[24,45,8,32]{3,2,0,1:T(8,128)(2,1)} reshape(bf16[24,45,256]{2,0,1:T(8,128)(2,1)} %param.25) | data formatting | bytes 1105920 | tf_op jit(solution)/shard_map/reshape | solution.py:94
  26.2 4.9 %copy.97 = bf16[24,45,8,32,1]{1,3,0,4,2:T(8,128)(2,1)} copy(bf16[24,45,8,32,1]{3,2,0,1,4:T(8,128)(2,1)} %bitcast.110) | data formatting | bytes 1105920 | tf_op jit(solution)/shard_map/reshape | solution.py:94
  31.3 1.6 collective-permute-start.6
  32.9 1.5 collective-permute-start.7
  34.4 1.2 fusion.14
  35.6 2.1 collective-permute-done.7
  37.7 1.2 fusion.7
  38.9 1.2 fusion.4
  40.4 3.7 %fusion = bf16[24,4,45,8,32]{2,4,0,1,3:T(8,128)(2,1)} fusion(f32[24,4,45,8]{2,0,1,3:T(8,128)S(1)} %copy.69, bf16[24,45,8,32,1]{1,3,0,4,2:T(8,128)(2,1)S(1)} %copy-done.15, bf16[8,4,32,32]{3,2,1,0:T(8,128)(2,1)S(1)} %copy-done), kind=kOutput, calls=%fused_computation.1 | convolution fusion | flops 72990720 | bytes 2968576 | tf_op jit(solution)/shard_map/ijgo,gbco->ibjgc/dot_general | solution.py:100
  44.1 12.5 %copy.111 = bf16[24,4,45,8,32]{4,3,2,1,0:T(8,128)(2,1)} copy(bf16[24,4,45,8,32]{2,4,0,1,3:T(8,128)(2,1)} %fusion) | data formatting | bytes 4423680 | tf_op jit(solution)/shard_map/reshape | solution.py:104
  56.6 10.6 %reshape.294 = bf16[24,4,45,256]{3,2,1,0:T(8,128)(2,1)S(1)} reshape(bf16[24,4,45,8,32]{4,3,2,1,0:T(8,128)(2,1)} %copy.111) | data formatting | bytes 4423680 | tf_op jit(solution)/shard_map/reshape | solution.py:104
  67.2 1.9 convolution_bitcast_fusion
  69.2 1.1 copy-done.6
  70.3 0.8 fusion.1
  71.5 2.1 constant_dynamic-update-slice_fusion
  73.6 1.2 copy-done.1
  74.9 1.3 collective-permute-start.8
  76.3 3.8 %collective-permute-start.1 = (bf16[24,8,256]{2,1,0:T(8,128)(2,1)S(1)}, bf16[24,8,256]{2,1,0:T(8,128)(2,1)S(1)}, u32[]{:S(2)}, u32[]{:S(2)}) collective-permute-start(bf16[24,8,256]{2,1,0:T(8,128)(2,1)S(1)} %get-tuple-element.106), channel_id=1, source_target_pairs={{1,0},{2,1},{3,2},{0,3},{5,4},{6,5},{7,6},{4,7},{9,8},{10,9},{11,1... | collective-permute-start | bytes 294920 | tf_op jit(solution)/shard_map/ppermute | solution.py:18
  80.3 3.2 %mul.45 = f32[24,45,8,32]{3,2,0,1:T(8,128)} broadcast(f32[24,45,8]{2,0,1:T(8,128)S(1)} %copy.82), dimensions={0,1,2} | broadcast | bytes 1140480 | tf_op jit(solution)/shard_map/mul | solution.py:128
  83.5 4.5 %mul.46 = f32[24,45,256]{2,0,1:T(8,128)} reshape(f32[24,45,8,32]{3,2,0,1:T(8,128)} %mul.45) | data formatting | bytes 2211840 | tf_op jit(solution)/shard_map/mul | solution.py:128
  88.2 1.0 fusion.52
  89.1 4.3 %collective-permute-start.9 = (f32[1,61,256]{2,1,0:T(8,128)S(1)}, f32[1,61,256]{2,1,0:T(8,128)S(1)}, u32[]{:S(2)}, u32[]{:S(2)}) collective-permute-start(f32[1,61,256]{2,1,0:T(8,128)S(1)} %get-tuple-element.101), channel_id=1, source_target_pairs={{0,4},{4,8},{8,12},{12,16},{16,20},{20,24},{24,28},{1,5},{5,9},{9,... | collective-permute-start | bytes 187400 | tf_op jit(solution)/shard_map/ppermute | solution.py:26
  93.6 1.3 collective-permute-start.3
  94.9 4.8 %collective-permute-start.2 = (bf16[1,61,256]{2,1,0:T(8,128)(2,1)S(1)}, bf16[1,61,256]{2,1,0:T(8,128)(2,1)S(1)}, u32[]{:S(2)}, u32[]{:S(2)}) collective-permute-start(bf16[1,61,256]{2,1,0:T(8,128)(2,1)S(1)} %get-tuple-element.104), channel_id=1, source_target_pairs={{0,4},{4,8},{8,12},{12,16},{16,20},{20,24},{24,28},{1,5},{5,9},{9,... | collective-permute-start | bytes 93704 | tf_op jit(solution)/shard_map/ppermute | solution.py:15
  99.8 0.8 fusion.16
  100.6 1.1 slice.284
  103.2 3.0 add_add_fusion
  106.2 11.7 %reshape.293 = f32[24,4,45,8,32]{4,3,2,1,0:T(8,128)} reshape(f32[24,4,45,256]{3,2,1,0:T(8,128)} %add_add_fusion) | data formatting | bytes 8847360 | tf_op jit(solution)/shard_map/reshape | solution.py:86
  117.9 17.1 %copy.70 = f32[24,4,45,8,32]{2,4,0,1,3:T(8,128)} copy(f32[24,4,45,8,32]{4,3,2,1,0:T(8,128)} %reshape.293) | data formatting | bytes 8847360 | tf_op jit(solution)/shard_map/reshape | solution.py:86
  135.0 9.5 %divide_convert_fusion = bf16[24,4,45,8,32]{2,4,0,1,3:T(8,128)(2,1)} fusion(f32[24,4,45,8,32]{2,4,0,1,3:T(8,128)} %copy.70, f32[24,4,45,8]{2,0,1,3:T(8,128)S(1)} %copy-done.18), kind=kLoop, calls=%fused_computation.2 | loop fusion | flops 2211840 | bytes 6773760 | tf_op jit(solution)/shard_map/convert_element_type | solution.py:88
  144.5 5.4 %convolution_bitcast_fusion.1 = f32[8,4,32,32]{3,2,1,0:T(8,128)} fusion(bf16[24,4,45,8,32]{2,4,0,1,3:T(8,128)(2,1)} %divide_convert_fusion, bf16[24,45,8,32,1]{1,3,0,4,2:T(8,128)(2,1)S(1)} %copy-done.16), kind=kOutput, calls=%fused_computation.11 | convolution fusion | flops 70778880 | bytes 2895872 | tf_op jit(solution)/shard_map/ibjgc,ijgo->gbco/dot_general | solution.py:95
  149.8 4.9 %fusion.2 = bf16[24,45,8,32]{1,3,0,2:T(8,128)(2,1)} fusion(bf16[24,4,45,8,32]{2,4,0,1,3:T(8,128)(2,1)} %divide_convert_fusion, bf16[8,4,32,32]{3,2,1,0:T(8,128)(2,1)S(1)} %copy-done), kind=kOutput, calls=%fused_computation.9 | convolution fusion | flops 71055360 | bytes 2830336 | tf_op jit(solution)/shard_map/ibjgc,gbco->ijgo/dot_general | solution.py:90
  154.8 5.2 %copy.73 = bf16[24,45,8,32]{3,2,0,1:T(8,128)(2,1)S(1)} copy(bf16[24,45,8,32]{1,3,0,2:T(8,128)(2,1)} %fusion.2) | data formatting | bytes 1105920 | tf_op jit(solution)/shard_map/convert_element_type | solution.py:92
  160.0 2.3 convert_element_type.47
  162.4 1.3 fusion.51
  163.7 1.4 collective-permute-start.11
  165.1 121.7 %all-reduce.3.cloned.1.call-done = f32[8,4,32,32]{3,2,1,0:T(8,128)} async-done(((f32[8,4,32,32]{3,2,1,0:T(8,128)}), f32[8,4,32,32]{3,2,1,0:T(8,128)}) %all-reduce.3.cloned.1.call-update) | async-done | bytes 131088 | tf_op jit(solution)/shard_map/psum | solution.py:99
  286.7 1.9 broadcast_multiply_fusion
  289.4 1.0 copy.85
  (77 shorter events, 4.8 us)
Async XLA Ops:
  7.2 33.2 %copy-start = (bf16[8,4,32,32]{3,2,1,0:T(8,128)(2,1)S(1)}, bf16[8,4,32,32]{3,2,1,0:T(8,128)(2,1)}, u32[]{:S(2)}) copy-start(bf16[8,4,32,32]{3,2,1,0:T(8,128)(2,1)} %param.24) | copy-start | bytes 196612
  7.2 279.5 %all-reduce.3.cloned.1.call-start = ((), (), s32[]{:S(2)}) async-start(), calls=%async_computation | async-start | bytes 1048576 | tf_op jit(solution)/shard_map/psum | solution.py:99
  8.2 22.9 %collective-permute-start.4 = (bf16[24,8,8]{1,2,0:T(8,128)(2,1)S(1)}, bf16[24,8,8]{1,2,0:T(8,128)(2,1)S(1)}, u32[]{:S(2)}, u32[]{:S(2)}) collective-permute-start(bf16[24,8,8]{1,2,0:T(8,128)(2,1)S(1)} %get-tuple-element.109), channel_id=1, source_target_pairs={{0,1},{1,2},{2,3},{3,0},{4,5},{5,6},{6,7},{7,4},{8,9},{9,10},{10,1... | collective-permute-start | bytes 9224 | tf_op jit(solution)/shard_map/ppermute | solution.py:15
  11.3 19.8 %collective-permute-start.5 = (bf16[24,8,8]{1,2,0:T(8,128)(2,1)S(1)}, bf16[24,8,8]{1,2,0:T(8,128)(2,1)S(1)}, u32[]{:S(2)}, u32[]{:S(2)}) collective-permute-start(bf16[24,8,8]{1,2,0:T(8,128)(2,1)S(1)} %get-tuple-element.110), channel_id=1, source_target_pairs={{1,0},{2,1},{3,2},{0,3},{5,4},{6,5},{7,6},{4,7},{9,8},{10,9},{11,1... | collective-permute-start | bytes 9224 | tf_op jit(solution)/shard_map/ppermute | solution.py:18
  20.5 1.6 copy-start.14
  20.5 1.6 copy-start.19
  22.1 12.2 %copy-start.5 = (bf16[24,4,61,45]{2,0,3,1:T(8,128)(2,1)}, bf16[24,4,61,45]{2,0,3,1:T(8,128)(2,1)S(1)}, u32[]{:S(2)}) copy-start(bf16[24,4,61,45]{2,0,3,1:T(8,128)(2,1)S(1)} %get-tuple-element.97) | copy-start | bytes 1581124
  22.1 16.8 %copy-start.3 = (bf16[24,4,61,45]{2,0,3,1:T(8,128)(2,1)}, bf16[24,4,61,45]{2,0,3,1:T(8,128)(2,1)S(1)}, u32[]{:S(2)}) copy-start(bf16[24,4,61,45]{2,0,3,1:T(8,128)(2,1)S(1)} %get-tuple-element.98) | copy-start | bytes 1581124
  31.2 6.5 %copy-start.8 = (bf16[24,4,61,45]{2,0,3,1:T(8,128)(2,1)S(1)}, bf16[24,4,61,45]{2,0,3,1:T(8,128)(2,1)}, u32[]{:S(2)}) copy-start(bf16[24,4,61,45]{2,0,3,1:T(8,128)(2,1)} %get-tuple-element.96) | copy-start | bytes 1581124
  31.3 7.6 %collective-permute-start.6 = (bf16[1,61,8]{1,2,0:T(8,128)(2,1)S(1)}, bf16[1,61,8]{1,2,0:T(8,128)(2,1)S(1)}, u32[]{:S(2)}, u32[]{:S(2)}) collective-permute-start(bf16[1,61,8]{1,2,0:T(8,128)(2,1)S(1)} %get-tuple-element.107), channel_id=1, source_target_pairs={{0,4},{4,8},{8,12},{12,16},{16,20},{20,24},{24,28},{1,5},{5,9},{9,... | collective-permute-start | bytes 2936 | tf_op jit(solution)/shard_map/ppermute | solution.py:15
  32.9 4.8 %collective-permute-start.7 = (bf16[1,61,8]{1,2,0:T(8,128)(2,1)S(1)}, bf16[1,61,8]{1,2,0:T(8,128)(2,1)S(1)}, u32[]{:S(2)}, u32[]{:S(2)}) collective-permute-start(bf16[1,61,8]{1,2,0:T(8,128)(2,1)S(1)} %get-tuple-element.108), channel_id=1, source_target_pairs={{4,0},{8,4},{12,8},{16,12},{20,16},{24,20},{28,24},{5,1},{9,5},{13... | collective-permute-start | bytes 2936 | tf_op jit(solution)/shard_map/ppermute | solution.py:18
  38.9 1.5 copy-start.15
  40.4 3.7 %copy-start.17 = (f32[24,4,45,8]{2,0,1,3:T(8,128)}, f32[24,4,45,8]{2,0,1,3:T(8,128)S(1)}, u32[]{:S(2)}) copy-start(f32[24,4,45,8]{2,0,1,3:T(8,128)S(1)} %copy.69) | copy-start | bytes 414724
  69.1 1.2 copy-start.6
  70.3 1.2 copy-start.9
  73.6 1.2 copy-start.1
  74.9 13.3 %collective-permute-start.8 = (f32[1,61,256]{2,1,0:T(8,128)S(1)}, f32[1,61,256]{2,1,0:T(8,128)S(1)}, u32[]{:S(2)}, u32[]{:S(2)}) collective-permute-start(f32[1,61,256]{2,1,0:T(8,128)S(1)} %slice.281), channel_id=1, source_target_pairs={{4,0},{8,4},{12,8},{16,12},{20,16},{24,20},{28,24},{5,1},{9,5},{13... | collective-permute-start | bytes 187400 | tf_op jit(solution)/shard_map/ppermute | solution.py:26
  76.2 17.3 %collective-permute-start = (bf16[24,8,256]{2,1,0:T(8,128)(2,1)S(1)}, bf16[24,8,256]{2,1,0:T(8,128)(2,1)S(1)}, u32[]{:S(2)}, u32[]{:S(2)}) collective-permute-start(bf16[24,8,256]{2,1,0:T(8,128)(2,1)S(1)} %get-tuple-element.105), channel_id=1, source_target_pairs={{0,1},{1,2},{2,3},{3,0},{4,5},{5,6},{6,7},{7,4},{8,9},{9,10},{10,1... | collective-permute-start | bytes 294920 | tf_op jit(solution)/shard_map/ppermute | solution.py:15
  76.3 17.2 %collective-permute-start.1 = (bf16[24,8,256]{2,1,0:T(8,128)(2,1)S(1)}, bf16[24,8,256]{2,1,0:T(8,128)(2,1)S(1)}, u32[]{:S(2)}, u32[]{:S(2)}) collective-permute-start(bf16[24,8,256]{2,1,0:T(8,128)(2,1)S(1)} %get-tuple-element.106), channel_id=1, source_target_pairs={{1,0},{2,1},{3,2},{0,3},{5,4},{6,5},{7,6},{4,7},{9,8},{10,9},{11,1... | collective-permute-start | bytes 294920 | tf_op jit(solution)/shard_map/ppermute | solution.py:18
  83.5 4.5 %copy-start.2 = (f32[26,61,256]{2,1,0:T(8,128)S(1)}, f32[26,61,256]{2,1,0:T(8,128)}, u32[]{:S(2)}) copy-start(f32[26,61,256]{2,1,0:T(8,128)} %copy-done.1) | copy-start | bytes 4872196
  88.1 11.6 %copy-start.7 = (bf16[24,4,61,45]{2,0,3,1:T(8,128)(2,1)S(1)}, bf16[24,4,61,45]{2,0,3,1:T(8,128)(2,1)}, u32[]{:S(2)}) copy-start(bf16[24,4,61,45]{2,0,3,1:T(8,128)(2,1)} %copy-done.5) | copy-start | bytes 1581124
  89.1 11.4 %collective-permute-start.9 = (f32[1,61,256]{2,1,0:T(8,128)S(1)}, f32[1,61,256]{2,1,0:T(8,128)S(1)}, u32[]{:S(2)}, u32[]{:S(2)}) collective-permute-start(f32[1,61,256]{2,1,0:T(8,128)S(1)} %get-tuple-element.101), channel_id=1, source_target_pairs={{0,4},{4,8},{8,12},{12,16},{16,20},{20,24},{24,28},{1,5},{5,9},{9,... | collective-permute-start | bytes 187400 | tf_op jit(solution)/shard_map/ppermute | solution.py:26
  93.6 9.6 %collective-permute-start.3 = (bf16[1,61,256]{2,1,0:T(8,128)(2,1)S(1)}, bf16[1,61,256]{2,1,0:T(8,128)(2,1)S(1)}, u32[]{:S(2)}, u32[]{:S(2)}) collective-permute-start(bf16[1,61,256]{2,1,0:T(8,128)(2,1)S(1)} %get-tuple-element.103), channel_id=1, source_target_pairs={{4,0},{8,4},{12,8},{16,12},{20,16},{24,20},{28,24},{5,1},{9,5},{13... | collective-permute-start | bytes 93704 | tf_op jit(solution)/shard_map/ppermute | solution.py:18
  94.9 6.8 %collective-permute-start.2 = (bf16[1,61,256]{2,1,0:T(8,128)(2,1)S(1)}, bf16[1,61,256]{2,1,0:T(8,128)(2,1)S(1)}, u32[]{:S(2)}, u32[]{:S(2)}) collective-permute-start(bf16[1,61,256]{2,1,0:T(8,128)(2,1)S(1)} %get-tuple-element.104), channel_id=1, source_target_pairs={{0,4},{4,8},{8,12},{12,16},{16,20},{20,24},{24,28},{1,5},{5,9},{9,... | collective-permute-start | bytes 93704 | tf_op jit(solution)/shard_map/ppermute | solution.py:15
  100.5 1.9 copy-start.4
  100.6 2.7 copy-start.11
  101.7 1.5 copy-start.10
  101.7 60.6 %collective-permute-start.10 = (bf16[24,8,256]{2,1,0:T(8,128)(2,1)S(1)}, bf16[24,8,256]{2,1,0:T(8,128)(2,1)S(1)}, u32[]{:S(2)}, u32[]{:S(2)}) collective-permute-start(bf16[24,8,256]{2,1,0:T(8,128)(2,1)S(1)} %slice.305), channel_id=1, source_target_pairs={{0,3},{1,0},{2,1},{3,2},{4,7},{5,4},{6,5},{7,6},{8,11},{9,8},{10,9... | collective-permute-start | bytes 294920 | tf_op jit(solution)/shard_map/ppermute | solution.py:31
  117.9 17.1 %copy-start.18 = (f32[24,4,45,8]{2,0,1,3:T(8,128)S(1)}, f32[24,4,45,8]{2,0,1,3:T(8,128)}, u32[]{:S(2)}) copy-start(f32[24,4,45,8]{2,0,1,3:T(8,128)} %copy-done.17) | copy-start | bytes 414724
  135.0 9.5 %copy-start.16 = (bf16[24,45,8,32,1]{1,3,0,4,2:T(8,128)(2,1)S(1)}, bf16[24,45,8,32,1]{1,3,0,4,2:T(8,128)(2,1)}, u32[]{:S(2)}) copy-start(bf16[24,45,8,32,1]{1,3,0,4,2:T(8,128)(2,1)} %copy.97) | copy-start | bytes 1658884
  162.4 126.3 %copy-start.12 = (f32[24,45,256]{2,1,0:T(8,128)S(1)}, f32[24,45,256]{2,1,0:T(8,128)}, u32[]{:S(2)}) copy-start(f32[24,45,256]{2,1,0:T(8,128)} %slice.284) | copy-start | bytes 3317764
  162.4 126.6 %copy-start.13 = (f32[24,45,256]{2,0,1:T(8,128)S(1)}, f32[24,45,256]{2,0,1:T(8,128)}, u32[]{:S(2)}) copy-start(f32[24,45,256]{2,0,1:T(8,128)} %mul.46) | copy-start | bytes 3317764
  163.7 125.2 %collective-permute-start.11 = (f32[24,8,256]{2,1,0:T(8,128)S(1)}, f32[24,8,256]{2,1,0:T(8,128)S(1)}, u32[]{:S(2)}, u32[]{:S(2)}) collective-permute-start(f32[24,8,256]{2,1,0:T(8,128)S(1)} %get-tuple-element.99), channel_id=1, source_target_pairs={{0,1},{1,2},{2,3},{3,0},{4,5},{5,6},{6,7},{7,4},{8,9},{9,10},{10,1... | collective-permute-start | bytes 589832 | tf_op jit(solution)/shard_map/ppermute | solution.py:31
Sparse Core Ops, SparseCore 0:
  154.9 131.7 all-reduce.2
where the time goes:
time: 299 us; the launch traced here: 297 us
  waiting for transfers between devices  124 us (41%)
  local copies, waits for them, and re-layouts  89.6 us (30%)
  matrix products  27.9 us (9%)
  starting transfers between devices  25.3 us (8%)
  other arithmetic  16.3 us (5%)
  between operations  14.5 us (5%)
    psum x1, waiting for transfers between devices, local(): lax.psum(local_grad, ('lat', 'lon')) * (1.0 / math.sqrt(cell_count))  122 us
    reshape x2, local copies, waits for them, and re-layouts, local(): numerator.reshape(row_count, basis_count, col_count, group_count, group_w...  28.8 us
    reshape x2, local copies, waits for them, and re-layouts, local(): pulled = (back_prop / safe_denom[..., None]).astype(jnp.bfloat16).reshape...  23.1 us
    ppermute x4, starting transfers between devices, with_halo(): lax.ppermute(lax.slice_in_dim(block, block.shape[dim] - width, None, axis...  9.58 us
    convert_element_type x1, other arithmetic, local(): scaled = (numerator.reshape(row_count, basis_count, col_count, group_coun...  9.49 us
    reshape x2, local copies, waits for them, and re-layouts, local(): upstream = cotangent.reshape(row_count, col_count, group_count, group_width)  8.84 us
    ppermute x4, starting transfers between devices, with_halo(): lax.ppermute(lax.slice_in_dim(block, 0, width, axis=dim), axis, backward)  8.67 us
    mul x2, local copies, waits for them, and re-layouts, local(): gathered.reshape(row_count, col_count, group_count, group_width)  7.63 us
  transfers between devices with their start and end apart: 13, of which 2 were waited for; matrix products, arithmetic and copies ran while one was open for 32% of the time, Pallas kernels for 0%

commit v1 on v0

--- a/solution.py
+++ b/solution.py
@@ -96,7 +96,9 @@
         "ibjgc,ijgo->gbco", scaled, upstream, preferred_element_type=jnp.float32
     )
     cell_count = row_count * lax.axis_size("lat") * col_count * lax.axis_size("lon")
-    weight_grad = lax.psum(local_grad, ("lat", "lon")) * (1.0 / math.sqrt(cell_count))
+    weight_grad = jnp.sum(lax.all_gather(local_grad, ("lat", "lon")), axis=0) * (
+        1.0 / math.sqrt(cell_count)
+    )
     back_prop = jnp.einsum("ijgo,gbco->ibjgc", upstream, mixing, preferred_element_type=jnp.float32)
     pulled = (
         (back_prop / safe_denom[..., None])

time: 299 us -> 238 us (0.80)
  waiting for transfers between devices: 124 us -> 52.6 us
  other arithmetic: 16.3 us -> 24.5 us
  starting transfers between devices: 25.3 us -> 28.8 us
    psum x1 -> x0, waiting for transfers between devices: 122 us -> none  [local(): lax.psum(local_grad, ('lat', 'lon')) * (1.0 / math.sqrt(cell_count))]
    all_gather x0 -> x1, waiting for transfers between devices: none -> 46 us  [local(): lax.all_gather(local_grad, ('lat', 'lon'))]
    reduce_sum x0 -> x1, other arithmetic: none -> 7.94 us  [local(): jnp.sum(lax.all_gather(local_grad, ('lat', 'lon')), axis=0)]
    ppermute x2, waiting for transfers between devices: 0.01 us -> 4.06 us  [passed_along(): return lax.ppermute(block, axis, route)]
  transfers between devices with their start and end apart: 13 -> 13, of which waited for: 2 -> 4; matrix products, arithmetic and copies ran while one was open for 32% -> 35% of each run, Pallas kernels for 0% -> 0%
where the time goes in v1:
time: 238 us; the launch traced here: 237 us
  local copies, waits for them, and re-layouts  89.6 us (38%)
  waiting for transfers between devices  52.6 us (22%)
  starting transfers between devices  28.8 us (12%)
  matrix products  26.7 us (11%)
  other arithmetic  24.5 us (10%)
  between operations  14.4 us (6%)
    all_gather x1, waiting for transfers between devices, local(): lax.all_gather(local_grad, ('lat', 'lon'))  46 us
    reshape x2, local copies, waits for them, and re-layouts, local(): numerator.reshape(row_count, basis_count, col_count, group_count, group_w...  28.7 us
    reshape x2, local copies, waits for them, and re-layouts, local(): pulled = (back_prop / safe_denom[..., None]).astype(jnp.bfloat16).reshape...  23.3 us
    ppermute x4, starting transfers between devices, with_halo(): lax.ppermute(lax.slice_in_dim(block, block.shape[dim] - width, None, axis...  9.54 us
    convert_element_type x1, other arithmetic, local(): scaled = (numerator.reshape(row_count, basis_count, col_count, group_coun...  9.48 us
    reshape x2, local copies, waits for them, and re-layouts, local(): upstream = cotangent.reshape(row_count, col_count, group_count, group_width)  8.83 us
    ppermute x2, starting transfers between devices, passed_along(): return lax.ppermute(block, axis, route)  8.5 us
    ppermute x4, starting transfers between devices, with_halo(): lax.ppermute(lax.slice_in_dim(block, 0, width, axis=dim), axis, backward)  8.43 us
  transfers between devices with their start and end apart: 13, of which 4 were waited for; matrix products, arithmetic and copies ran while one was open for 35% of the time, Pallas kernels for 0%

profile of v1, /device:TPU:0, one launch (start us, length us, event | category | flops | bytes accessed | tf_op | source)
XLA Modules:
  0.0 236.5 jit_solution(11896406194372390302)
XLA Ops:
  7.2 0.9 convert_element_type.43
  8.9 3.1 %collective-permute-start.4 = (bf16[24,8,8]{1,2,0:T(8,128)(2,1)}, bf16[24,8,8]{1,2,0:T(8,128)(2,1)S(1)}, u32[]{:S(2)}, u32[]{:S(2)}) collective-permute-start(bf16[24,8,8]{1,2,0:T(8,128)(2,1)} %get-tuple-element.112), channel_id=1, source_target_pairs={{0,1},{1,2},{2,3},{3,0},{4,5},{5,6},{6,7},{7,4},{8,9},{9,10},{10,1... | collective-permute-start | bytes 9224 | tf_op jit(solution)/shard_map/ppermute | solution.py:15
  11.9 2.0 collective-permute-start.5
  14.2 1.4 mul.42
  15.6 1.5 mul.43
  17.2 1.3 copy_multiply_fusion.1
  19.1 3.8 %collective-permute-start.1 = (bf16[24,8,256]{2,1,0:T(8,128)(2,1)S(1)}, bf16[24,8,256]{2,1,0:T(8,128)(2,1)S(1)}, u32[]{:S(2)}, u32[]{:S(2)}) collective-permute-start(bf16[24,8,256]{2,1,0:T(8,128)(2,1)S(1)} %get-tuple-element.109), channel_id=1, source_target_pairs={{1,0},{2,1},{3,2},{0,3},{5,4},{6,5},{7,6},{4,7},{9,8},{10,9},{11,1... | collective-permute-start | bytes 294920 | tf_op jit(solution)/shard_map/ppermute | solution.py:18
  23.5 1.0 convolution_convert_fusion
  24.5 1.6 slice_bitcast_fusion
  26.1 3.9 %reshape.274 = bf16[24,45,8,32]{3,2,0,1:T(8,128)(2,1)} reshape(bf16[24,45,256]{2,0,1:T(8,128)(2,1)} %param.25) | data formatting | bytes 1105920 | tf_op jit(solution)/shard_map/reshape | solution.py:94
  30.0 4.9 %copy.125 = bf16[24,45,8,32,1]{1,3,0,4,2:T(8,128)(2,1)} copy(bf16[24,45,8,32,1]{3,2,0,1,4:T(8,128)(2,1)} %bitcast.112) | data formatting | bytes 1105920 | tf_op jit(solution)/shard_map/reshape | solution.py:94
  35.0 1.4 collective-permute-start.6
  36.5 1.3 collective-permute-start.7
  37.8 1.2 fusion.14
  39.0 2.5 %collective-permute-done.7 = bf16[1,61,8]{1,2,0:T(8,128)(2,1)S(1)} collective-permute-done((bf16[1,61,8]{1,2,0:T(8,128)(2,1)S(1)}, bf16[1,61,8]{1,2,0:T(8,128)(2,1)S(1)}, u32[]{:S(2)}, u32[]{:S(2)}) %collective-permute-start.7) | collective-permute-done | bytes 1008 | tf_op jit(solution)/shard_map/ppermute | solution.py:18
  41.5 1.2 fusion.7
  42.7 1.3 fusion.4
  43.9 1.0 copy.97
  45.1 1.3 collective-permute-start.3
  46.4 5.1 %collective-permute-start.2 = (bf16[1,61,256]{2,1,0:T(8,128)(2,1)S(1)}, bf16[1,61,256]{2,1,0:T(8,128)(2,1)S(1)}, u32[]{:S(2)}, u32[]{:S(2)}) collective-permute-start(bf16[1,61,256]{2,1,0:T(8,128)(2,1)S(1)} %get-tuple-element.107), channel_id=1, source_target_pairs={{0,4},{4,8},{8,12},{12,16},{16,20},{20,24},{24,28},{1,5},{5,9},{9,... | collective-permute-start | bytes 93704 | tf_op jit(solution)/shard_map/ppermute | solution.py:15
  53.0 3.0 %add_add_fusion = f32[24,4,45,256]{3,2,1,0:T(8,128)} fusion(f32[24,4,45,256]{3,2,1,0:T(8,128)S(1)} %fusion.20, f32[24,4,45,256]{3,2,1,0:T(8,128)S(1)} %fusion.16, bf16[24,4,61,45]{2,0,3,1:T(8,128)(2,1)S(1)} %copy-done.4, bf16[1,61,256]{2,1,0:T(8,128)(2,1)S(1)} %collective-permute-done.3, bf16[24,8,256]{2,1,0:T(8,128)(2,1)S(1)} %collective-permute-done.1, ...), kind=kOutput, calls=%fused_computation.3 | convolution fusion | flops 140132352 | bytes 14578880 | tf_op jit(solution)/shard_map/ibpj,ipc->ibjc/dot_general | solution.py:72
  56.0 11.6 %reshape.294 = f32[24,4,45,8,32]{4,3,2,1,0:T(8,128)} reshape(f32[24,4,45,256]{3,2,1,0:T(8,128)} %add_add_fusion) | data formatting | bytes 8847360 | tf_op jit(solution)/shard_map/reshape | solution.py:86
  67.6 17.1 %copy.98 = f32[24,4,45,8,32]{2,4,0,1,3:T(8,128)} copy(f32[24,4,45,8,32]{4,3,2,1,0:T(8,128)} %reshape.294) | data formatting | bytes 8847360 | tf_op jit(solution)/shard_map/reshape | solution.py:86
  84.7 9.5 %divide_convert_fusion = bf16[24,4,45,8,32]{2,4,0,1,3:T(8,128)(2,1)} fusion(f32[24,4,45,8,32]{2,4,0,1,3:T(8,128)} %copy.98, f32[24,4,45,8]{2,0,1,3:T(8,128)S(1)} %copy-done.7), kind=kLoop, calls=%fused_computation.2 | loop fusion | flops 2211840 | bytes 6773760 | tf_op jit(solution)/shard_map/convert_element_type | solution.py:88
  94.1 5.4 %convolution_bitcast_fusion.1 = f32[8,4,32,32]{3,2,1,0:T(8,128)} fusion(bf16[24,4,45,8,32]{2,4,0,1,3:T(8,128)(2,1)} %divide_convert_fusion, bf16[24,45,8,32,1]{1,3,0,4,2:T(8,128)(2,1)S(1)} %copy-done.6), kind=kOutput, calls=%fused_computation.11 | convolution fusion | flops 70778880 | bytes 2895872 | tf_op jit(solution)/shard_map/ibjgc,ijgo->gbco/dot_general | solution.py:95
  99.5 3.6 %fusion = bf16[24,4,45,8,32]{2,4,0,1,3:T(8,128)(2,1)} fusion(f32[24,4,45,8]{2,0,1,3:T(8,128)S(1)} %copy-done.7, bf16[24,45,8,32,1]{1,3,0,4,2:T(8,128)(2,1)S(1)} %copy-done.6, bf16[8,4,32,32]{3,2,1,0:T(8,128)(2,1)S(1)} %copy-done), kind=kOutput, calls=%fused_computation.1 | convolution fusion | flops 72990720 | bytes 2968576 | tf_op jit(solution)/shard_map/ijgo,gbco->ibjgc/dot_general | solution.py:102
  103.1 12.7 %copy.139 = bf16[24,4,45,8,32]{4,3,2,1,0:T(8,128)(2,1)} copy(bf16[24,4,45,8,32]{2,4,0,1,3:T(8,128)(2,1)} %fusion) | data formatting | bytes 4423680 | tf_op jit(solution)/shard_map/reshape | solution.py:106
  115.8 10.6 %reshape.295 = bf16[24,4,45,256]{3,2,1,0:T(8,128)(2,1)S(1)} reshape(bf16[24,4,45,8,32]{4,3,2,1,0:T(8,128)(2,1)} %copy.139) | data formatting | bytes 4423680 | tf_op jit(solution)/shard_map/reshape | solution.py:106
  126.4 1.9 convolution_bitcast_fusion
  128.4 1.1 copy-done.3
  130.7 0.9 constant_dynamic-update-slice_fusion
  131.7 1.3 collective-permute-start.8
  133.1 3.2 %collective-permute-done.8 = f32[1,61,256]{2,1,0:T(8,128)S(1)} collective-permute-done((f32[1,61,256]{2,1,0:T(8,128)S(1)}, f32[1,61,256]{2,1,0:T(8,128)S(1)}, u32[]{:S(2)}, u32[]{:S(2)}) %collective-permute-start.8) | collective-permute-done | bytes 62496 | tf_op jit(solution)/shard_map/ppermute | solution.py:26
  136.3 7.2 %collective-permute-start.9 = (f32[1,61,256]{2,1,0:T(8,128)S(1)}, f32[1,61,256]{2,1,0:T(8,128)S(1)}, u32[]{:S(2)}, u32[]{:S(2)}) collective-permute-start(f32[1,61,256]{2,1,0:T(8,128)S(1)} %get-tuple-element.104), channel_id=1, source_target_pairs={{0,4},{4,8},{8,12},{12,16},{16,20},{20,24},{24,28},{1,5},{5,9},{9,... | collective-permute-start | bytes 187400 | tf_op jit(solution)/shard_map/ppermute | solution.py:26
  143.6 0.9 collective-permute-done.9
  145.0 3.1 %mul.45 = f32[24,45,8,32]{3,2,0,1:T(8,128)} broadcast(f32[24,45,8]{2,0,1:T(8,128)S(1)} %copy.110), dimensions={0,1,2} | broadcast | bytes 1140480 | tf_op jit(solution)/shard_map/mul | solution.py:130
  148.2 4.4 %mul.46 = f32[24,45,256]{2,0,1:T(8,128)} reshape(f32[24,45,8,32]{3,2,0,1:T(8,128)} %mul.45) | data formatting | bytes 2211840 | tf_op jit(solution)/shard_map/mul | solution.py:130
  152.6 1.1 slice.284
  153.7 2.0 collective-permute-start.11
  155.8 4.9 %fusion.2 = bf16[24,45,8,32]{1,3,0,2:T(8,128)(2,1)} fusion(bf16[24,4,45,8,32]{2,4,0,1,3:T(8,128)(2,1)} %divide_convert_fusion, bf16[8,4,32,32]{3,2,1,0:T(8,128)(2,1)S(1)} %copy-done), kind=kOutput, calls=%fused_computation.9 | convolution fusion | flops 71055360 | bytes 2830336 | tf_op jit(solution)/shard_map/ibjgc,gbco->ijgo/dot_general | solution.py:90
  160.7 5.2 %copy.101 = bf16[24,45,8,32]{3,2,0,1:T(8,128)(2,1)S(1)} copy(bf16[24,45,8,32]{1,3,0,2:T(8,128)(2,1)} %fusion.2) | data formatting | bytes 1105920 | tf_op jit(solution)/shard_map/convert_element_type | solution.py:92
  165.9 2.3 convert_element_type.47
  168.2 2.0 scatter-add.31
  170.2 1.7 fusion.34
  171.9 2.0 fusion.5
  173.8 1.0 copy.113
  174.8 46.0 %all-gather.3.cloned.1.call-done = f32[256,4,32,32]{3,2,1,0:T(8,128)} async-done(((f32[8,4,32,32]{3,2,1,0:T(8,128)}), f32[256,4,32,32]{3,2,1,0:T(8,128)}) %all-gather.3.cloned.1.call-update) | async-done | bytes 4194320 | tf_op jit(solution)/shard_map/all_gather | solution.py:99
  220.9 7.9 %reduce_sum.9 = f32[8,4,32,32]{3,2,1,0:T(8,128)S(1)} reduce(f32[32,8,4,32,32]{4,3,2,1,0:T(8,128)} %bitcast.111, f32[]{:T(128)} %constant.201.clone.1), dimensions={0}, to_apply=%region_0.0 | reduce | flops 1015808 | bytes 4325380 | tf_op jit(solution)/shard_map/reduce_sum | solution.py:99
  (58 shorter events, 7.1 us)
Async XLA Ops:
  7.2 92.4 %copy-start = (bf16[8,4,32,32]{3,2,1,0:T(8,128)(2,1)S(1)}, bf16[8,4,32,32]{3,2,1,0:T(8,128)(2,1)}, u32[]{:S(2)}) copy-start(bf16[8,4,32,32]{3,2,1,0:T(8,128)(2,1)} %param.24) | copy-start | bytes 196612
  7.2 213.7 %all-gather.3.cloned.1.call-start = ((), (), s32[]{:S(2)}) async-start(), calls=%async_computation | async-start | bytes 17301504 | tf_op jit(solution)/shard_map/all_gather | solution.py:99
  8.9 26.0 %collective-permute-start.4 = (bf16[24,8,8]{1,2,0:T(8,128)(2,1)}, bf16[24,8,8]{1,2,0:T(8,128)(2,1)S(1)}, u32[]{:S(2)}, u32[]{:S(2)}) collective-permute-start(bf16[24,8,8]{1,2,0:T(8,128)(2,1)} %get-tuple-element.112), channel_id=1, source_target_pairs={{0,1},{1,2},{2,3},{3,0},{4,5},{5,6},{6,7},{7,4},{8,9},{9,10},{10,1... | collective-permute-start | bytes 9224 | tf_op jit(solution)/shard_map/ppermute | solution.py:15
  11.9 23.0 %collective-permute-start.5 = (bf16[24,8,8]{1,2,0:T(8,128)(2,1)S(1)}, bf16[24,8,8]{1,2,0:T(8,128)(2,1)S(1)}, u32[]{:S(2)}, u32[]{:S(2)}) collective-permute-start(bf16[24,8,8]{1,2,0:T(8,128)(2,1)S(1)} %get-tuple-element.113), channel_id=1, source_target_pairs={{1,0},{2,1},{3,2},{0,3},{5,4},{6,5},{7,6},{4,7},{9,8},{10,9},{11,1... | collective-permute-start | bytes 9224 | tf_op jit(solution)/shard_map/ppermute | solution.py:18
  17.1 5.8 %copy-start.9 = (s32[192]{0:T(256)S(1)}, s32[192]{0:T(256)}, u32[]{:S(2)}) copy-start(s32[192]{0:T(256)} %param.23) | copy-start | bytes 2308
  17.1 6.0 %copy-start.8 = (bf16[192,4,3,17]{0,1,3,2:T(4,128)(2,1)S(1)}, bf16[192,4,3,17]{0,1,3,2:T(4,128)(2,1)}, u32[]{:S(2)}) copy-start(bf16[192,4,3,17]{0,1,3,2:T(4,128)(2,1)} %param.22) | copy-start | bytes 235012
  19.1 25.9 %collective-permute-start = (bf16[24,8,256]{2,1,0:T(8,128)(2,1)}, bf16[24,8,256]{2,1,0:T(8,128)(2,1)S(1)}, u32[]{:S(2)}, u32[]{:S(2)}) collective-permute-start(bf16[24,8,256]{2,1,0:T(8,128)(2,1)} %get-tuple-element.108), channel_id=1, source_target_pairs={{0,1},{1,2},{2,3},{3,0},{4,5},{5,6},{6,7},{7,4},{8,9},{9,10},{10,1... | collective-permute-start | bytes 294920 | tf_op jit(solution)/shard_map/ppermute | solution.py:15
  19.1 25.9 %collective-permute-start.1 = (bf16[24,8,256]{2,1,0:T(8,128)(2,1)S(1)}, bf16[24,8,256]{2,1,0:T(8,128)(2,1)S(1)}, u32[]{:S(2)}, u32[]{:S(2)}) collective-permute-start(bf16[24,8,256]{2,1,0:T(8,128)(2,1)S(1)} %get-tuple-element.109), channel_id=1, source_target_pairs={{1,0},{2,1},{3,2},{0,3},{5,4},{6,5},{7,6},{4,7},{9,8},{10,9},{11,1... | collective-permute-start | bytes 294920 | tf_op jit(solution)/shard_map/ppermute | solution.py:18
  26.1 25.4 %copy-start.2 = (bf16[24,4,61,45]{2,0,3,1:T(8,128)(2,1)}, bf16[24,4,61,45]{2,0,3,1:T(8,128)(2,1)S(1)}, u32[]{:S(2)}) copy-start(bf16[24,4,61,45]{2,0,3,1:T(8,128)(2,1)S(1)} %get-tuple-element.100) | copy-start | bytes 1581124
  26.1 26.2 %copy-start.1 = (bf16[24,4,61,45]{2,0,3,1:T(8,128)(2,1)}, bf16[24,4,61,45]{2,0,3,1:T(8,128)(2,1)S(1)}, u32[]{:S(2)}) copy-start(bf16[24,4,61,45]{2,0,3,1:T(8,128)(2,1)S(1)} %get-tuple-element.101) | copy-start | bytes 1581124
  34.9 6.6 %copy-start.4 = (bf16[24,4,61,45]{2,0,3,1:T(8,128)(2,1)S(1)}, bf16[24,4,61,45]{2,0,3,1:T(8,128)(2,1)}, u32[]{:S(2)}) copy-start(bf16[24,4,61,45]{2,0,3,1:T(8,128)(2,1)} %get-tuple-element.99) | copy-start | bytes 1581124
  35.0 7.7 %collective-permute-start.6 = (bf16[1,61,8]{1,2,0:T(8,128)(2,1)S(1)}, bf16[1,61,8]{1,2,0:T(8,128)(2,1)S(1)}, u32[]{:S(2)}, u32[]{:S(2)}) collective-permute-start(bf16[1,61,8]{1,2,0:T(8,128)(2,1)S(1)} %get-tuple-element.110), channel_id=1, source_target_pairs={{0,4},{4,8},{8,12},{12,16},{16,20},{20,24},{24,28},{1,5},{5,9},{9,... | collective-permute-start | bytes 2936 | tf_op jit(solution)/shard_map/ppermute | solution.py:15
  36.5 5.0 %collective-permute-start.7 = (bf16[1,61,8]{1,2,0:T(8,128)(2,1)S(1)}, bf16[1,61,8]{1,2,0:T(8,128)(2,1)S(1)}, u32[]{:S(2)}, u32[]{:S(2)}) collective-permute-start(bf16[1,61,8]{1,2,0:T(8,128)(2,1)S(1)} %get-tuple-element.111), channel_id=1, source_target_pairs={{4,0},{8,4},{12,8},{16,12},{20,16},{24,20},{28,24},{5,1},{9,5},{13... | collective-permute-start | bytes 2936 | tf_op jit(solution)/shard_map/ppermute | solution.py:18
  45.1 7.9 %collective-permute-start.3 = (bf16[1,61,256]{2,1,0:T(8,128)(2,1)S(1)}, bf16[1,61,256]{2,1,0:T(8,128)(2,1)S(1)}, u32[]{:S(2)}, u32[]{:S(2)}) collective-permute-start(bf16[1,61,256]{2,1,0:T(8,128)(2,1)S(1)} %get-tuple-element.106), channel_id=1, source_target_pairs={{4,0},{8,4},{12,8},{16,12},{20,16},{24,20},{28,24},{5,1},{9,5},{13... | collective-permute-start | bytes 93704 | tf_op jit(solution)/shard_map/ppermute | solution.py:18
  46.4 5.9 %collective-permute-start.2 = (bf16[1,61,256]{2,1,0:T(8,128)(2,1)S(1)}, bf16[1,61,256]{2,1,0:T(8,128)(2,1)S(1)}, u32[]{:S(2)}, u32[]{:S(2)}) collective-permute-start(bf16[1,61,256]{2,1,0:T(8,128)(2,1)S(1)} %get-tuple-element.107), channel_id=1, source_target_pairs={{0,4},{4,8},{8,12},{12,16},{16,20},{20,24},{24,28},{1,5},{5,9},{9,... | collective-permute-start | bytes 93704 | tf_op jit(solution)/shard_map/ppermute | solution.py:15
  67.6 17.1 %copy-start.7 = (f32[24,4,45,8]{2,0,1,3:T(8,128)S(1)}, f32[24,4,45,8]{2,0,1,3:T(8,128)}, u32[]{:S(2)}) copy-start(f32[24,4,45,8]{2,0,1,3:T(8,128)} %copy.97) | copy-start | bytes 414724
  84.7 9.5 %copy-start.6 = (bf16[24,45,8,32,1]{1,3,0,4,2:T(8,128)(2,1)S(1)}, bf16[24,45,8,32,1]{1,3,0,4,2:T(8,128)(2,1)}, u32[]{:S(2)}) copy-start(bf16[24,45,8,32,1]{1,3,0,4,2:T(8,128)(2,1)} %copy.125) | copy-start | bytes 1658884
  128.2 1.2 copy-start.3
  129.5 1.2 copy-start.5
  131.7 4.6 %collective-permute-start.8 = (f32[1,61,256]{2,1,0:T(8,128)S(1)}, f32[1,61,256]{2,1,0:T(8,128)S(1)}, u32[]{:S(2)}, u32[]{:S(2)}) collective-permute-start(f32[1,61,256]{2,1,0:T(8,128)S(1)} %slice.281), channel_id=1, source_target_pairs={{4,0},{8,4},{12,8},{16,12},{20,16},{24,20},{28,24},{5,1},{9,5},{13... | collective-permute-start | bytes 187400 | tf_op jit(solution)/shard_map/ppermute | solution.py:26
  136.3 8.1 %collective-permute-start.9 = (f32[1,61,256]{2,1,0:T(8,128)S(1)}, f32[1,61,256]{2,1,0:T(8,128)S(1)}, u32[]{:S(2)}, u32[]{:S(2)}) collective-permute-start(f32[1,61,256]{2,1,0:T(8,128)S(1)} %get-tuple-element.104), channel_id=1, source_target_pairs={{0,4},{4,8},{8,12},{12,16},{16,20},{20,24},{24,28},{1,5},{5,9},{9,... | collective-permute-start | bytes 187400 | tf_op jit(solution)/shard_map/ppermute | solution.py:26
  144.5 9.2 %collective-permute-start.10 = (bf16[24,8,256]{2,1,0:T(8,128)(2,1)S(1)}, bf16[24,8,256]{2,1,0:T(8,128)(2,1)S(1)}, u32[]{:S(2)}, u32[]{:S(2)}) collective-permute-start(bf16[24,8,256]{2,1,0:T(8,128)(2,1)S(1)} %slice.305), channel_id=1, source_target_pairs={{0,3},{1,0},{2,1},{3,2},{4,7},{5,4},{6,5},{7,6},{8,11},{9,8},{10,9... | collective-permute-start | bytes 294920 | tf_op jit(solution)/shard_map/ppermute | solution.py:31
  153.7 16.5 %collective-permute-start.11 = (f32[24,8,256]{2,1,0:T(8,128)S(1)}, f32[24,8,256]{2,1,0:T(8,128)S(1)}, u32[]{:S(2)}, u32[]{:S(2)}) collective-permute-start(f32[24,8,256]{2,1,0:T(8,128)S(1)} %get-tuple-element.102), channel_id=1, source_target_pairs={{0,1},{1,2},{2,3},{3,0},{4,5},{5,6},{6,7},{7,4},{8,9},{9,10},{10,1... | collective-permute-start | bytes 589832 | tf_op jit(solution)/shard_map/ppermute | solution.py:31
Sparse Core Ops, SparseCore 0:
  99.6 121.1 all-gather.2
